TPU v7x, 512 devices: a whole 4x4x16 slice. The times are simulated.
512 devices in a mesh: var: 16 (over x, z_lo), dp: 32 (over y, z_hi, core).
Axes of the slice: x: 4, y: 4, z: 16 (z_hi: 4, z_lo: 4; z = z_hi * 4 + z_lo), core: 2. Of those that a mesh axis runs over, the one named last changes fastest.
Arguments:
- fields: bfloat16 [32, 64, 32, 128], P('dp', 'var'), may hold values from -6 to 6
- kernels: bfloat16 [64, 16, 512], P('var'), may hold values from -1.5 to 1.5
- level_map: int32 [64], P('var'), may hold values 0 or 1
- norm_gain_vector: float32 [512], replicated, may hold values from 0.1 to 1.9
- w_in: bfloat16 [512, 2048], replicated, may hold values from -0.25 to 0.25
- w_out: bfloat16 [2048, 512], replicated, may hold values from -0.125 to 0.125
- cotangent: bfloat16 [32, 16, 256, 512], P('dp', None, 'var'), may hold values from -6 to 6
Outputs:
- block_out: bfloat16 [32, 16, 256, 512], P('dp', None, 'var')
- kernel_grad: float32 [64, 16, 512], P('var', None, 'dp')
Inputs may be any that keep to these rules, and one draw needn't show every extreme that they name: variable-level v belongs to pressure level v // 4 and enters its aggregate where level_map[v] is 1.
All inputs are finite; a program needn't handle non-finite values. No bound on the sum of `level_map` on one device may be relied on, other than what follows from the above.
Results may differ from a plain program's by a relative error of at most 0.013.
Values may be sent and summed in bfloat16 or wider, within the bound.
No kernel may reach another device: no remote copies, remote signals or barrier semaphores. Data moves between devices by JAX's collectives and lax.ppermute only.
A program may use at most 64 MiB of HBM per device.

v0:
```python
import jax
import jax.numpy as jnp
from jax import lax
from jax.sharding import PartitionSpec as P

PATCH = 4


def patches_of(images):
    batch, count_v, height, width = images.shape
    shaped = images.reshape(batch, count_v, height // PATCH, PATCH, width // PATCH, PATCH)
    return shaped.transpose(0, 1, 2, 4, 3, 5).reshape(
        batch, count_v, height // PATCH * (width // PATCH), PATCH * PATCH
    )


def block_pass(token_rows, grads, norm_gain_vector, w_in, w_out):
    width = token_rows.shape[-1]
    rows = token_rows.reshape(-1, width).astype(jnp.float32)
    mean_row = jnp.mean(rows, axis=1, keepdims=True)
    centered_rows = rows - mean_row
    reciprocal_std = lax.rsqrt(
        jnp.mean(centered_rows * centered_rows, axis=1, keepdims=True) + 1e-05
    )
    normalized_input = centered_rows * reciprocal_std
    normalized_rows = (normalized_input * norm_gain_vector).astype(jnp.bfloat16)
    pre = jnp.dot(normalized_rows, w_in, preferred_element_type=jnp.float32)
    hidden = jax.nn.gelu(pre, approximate=True).astype(jnp.bfloat16)
    output = (rows + jnp.dot(hidden, w_out, preferred_element_type=jnp.float32)).astype(
        jnp.bfloat16
    )
    gradient_rows = grads.reshape(-1, width)
    dhid = jnp.dot(gradient_rows, w_out.T, preferred_element_type=jnp.float32)
    gelu_back = jax.vjp(lambda value: jax.nn.gelu(value, approximate=True), pre)[1]
    dpre = gelu_back(dhid)[0].astype(jnp.bfloat16)
    dnorm = jnp.dot(dpre, w_in.T, preferred_element_type=jnp.float32)
    normalized_gradient = dnorm * norm_gain_vector
    token_gradient = gradient_rows.astype(jnp.float32) + reciprocal_std * (
        normalized_gradient
        - jnp.mean(normalized_gradient, axis=1, keepdims=True)
        - normalized_input * jnp.mean(normalized_gradient * normalized_input, axis=1, keepdims=True)
    )
    return (
        output.reshape(token_rows.shape),
        token_gradient.astype(jnp.bfloat16).reshape(token_rows.shape),
    )


def level_tables(level, weight, groups):
    onehot = (level[None, :] == jnp.arange(groups, dtype=jnp.int32)[:, None]).astype(
        jnp.float32
    ) * weight[None, :]
    inv = 1.0 / jnp.maximum(jnp.sum(onehot, axis=1), 1.0)
    return (onehot * inv[:, None], inv[level] * weight)


def local(fields, kernels, level_map, norm_gain_vector, w_in, w_out, cotangent):
    batch, var_local = (fields.shape[0], fields.shape[1])
    patch_inputs = patches_of(fields)
    tokens_all = patch_inputs.shape[2]
    scale = float(batch * lax.axis_size("dp") * tokens_all) ** (-0.5)
    own_level = jnp.zeros((var_local,), jnp.int32)
    own_assign, own_member = level_tables(own_level, level_map.astype(jnp.float32), 1)
    patch_embeddings = jnp.einsum(
        "bvnp,vpe->bvne", patch_inputs, kernels, preferred_element_type=jnp.float32
    )
    token_rows = jnp.einsum("lv,bvne->blne", own_assign, patch_embeddings).astype(jnp.bfloat16)
    row_tokens = lax.all_to_all(token_rows, "var", split_axis=2, concat_axis=1, tiled=True)
    block_out, token_gradient = block_pass(row_tokens, cotangent, norm_gain_vector, w_in, w_out)
    dlevel = lax.all_to_all(token_gradient, "var", split_axis=1, concat_axis=2, tiled=True)
    partial_grad = (
        jnp.einsum("bvnp,bne->vpe", patch_inputs, dlevel[:, 0], preferred_element_type=jnp.float32)
        * own_member[:, None, None]
    )
    kernel_grad = lax.psum_scatter(partial_grad, "dp", scatter_dimension=2, tiled=True) * scale
    return (block_out, kernel_grad)


def solution(mesh):
    placed = (
        P("dp", "var", None, None),
        P("var", None, None),
        P("var"),
        P(),
        P(),
        P(),
        P("dp", None, "var", None),
    )
    return jax.shard_map(
        local,
        mesh=mesh,
        in_specs=placed,
        out_specs=(P("dp", None, "var", None), P("var", None, "dp")),
        check_vma=False,
    )
```

profile of v0, /device:TPU:2, one launch (start us, length us, event | category | flops | bytes accessed | tf_op | source)
XLA Modules:
  0.0 183.3 jit_solution(2640362188607401655)
XLA Ops:
  7.2 1.4 convert_reduce_fusion.1
  9.3 3.0 %reshape.106 = bf16[1,4,8,4,32,4]{5,4,3,2,1,0:T(8,128)(2,1)S(1)} reshape(bf16[1,4,32,128]{3,2,1,0:T(8,128)(2,1)} %param.7) | data formatting | bytes 65536 | tf_op jit(solution)/shard_map/reshape | solution.py:11
  12.3 0.9 copy.14
  13.3 0.5 convolution_bitcast_fusion
  13.8 1.8 copy.18
  15.6 1.9 %fusion.47 = bf16[1,256,512]{2,0,1:T(2,128)(2,1)S(1)} fusion(bf16[4,256,512]{2,0,1:T(4,128)(2,1)} %copy.18, f32[]{:T(128)S(6)} %div.16, s32[4]{0:T(128)S(1)} %copy-done.4), kind=kOutput, calls=%fused_computation.62 | convolution fusion | flops 1048584 | bytes 1310740 | tf_op jit(solution)/shard_map/lv,bvne->blne/dot_general | solution.py:67
  17.6 0.4 copy.28
  18.0 0.5 broadcast.100
  18.5 2.3 %reduce.6 = bf16[256,512]{1,0:T(8,128)(2,1)S(1)} reduce(bf16[256,1,1,512]{3,2,1,0:T(2,128)(2,1)S(1)} %bitcast.92, bf16[]{:T(256)} %broadcast.100), dimensions={1,2}, to_apply=%bitcast.88.reduce_sub_computation | reduce | bytes 524290
  20.8 0.2 reshape.120
  21.0 17.0 %all_to_all.8 = bf16[16,2,4096]{2,1,0:T(2,128)(2,1)S(1)} all-to-all(bf16[16,2,4096]{2,1,0:T(2,128)(2,1)S(1)} %reshape.120), channel_id=1, replica_groups=mesh['var'=16,'dp'=32] {'var'}, dimensions={0} | all-to-all | bytes 524288 | tf_op jit(solution)/shard_map/all_to_all | solution.py:68
  38.0 0.3 reshape.121
  38.4 0.2 fusion.24
  38.7 2.1 %fusion.26 = f32[256,2048]{1,0:T(8,128)} fusion(bf16[512,2048]{1,0:T(8,128)(2,1)S(1)} %copy-done, bf16[1,1,256,512]{3,2,1,0:T(8,128)(2,1)S(1)} %get-tuple-element.5, f32[512]{0:T(512)S(1)} %copy-done.3, f32[256]{0:T(256)S(1)} %add_rsqrt_fusion, f32[256]{0:T(256)S(1)} %broadcast_multiply_fusion.3), kind=kOutput, calls=%fused_computation.35 | convolution fusion | flops 537526272 | bytes 4460544 | tf_op jit(solution)/shard_map/dot_general | solution.py:27
  40.8 4.7 %fusion.43 = (f32[256]{0:T(256)S(1)}, f32[256]{0:T(256)S(1)}, f32[256,512]{1,0:T(8,128)S(1)}) fusion(f32[256]{0:T(256)S(1)} %add_rsqrt_fusion, f32[256]{0:T(256)S(1)} %broadcast_multiply_fusion.3, bf16[1,1,256,512]{3,2,1,0:T(8,128)(2,1)S(1)} %get-tuple-element.5, f32[512]{0:T(512)S(1)} %copy-done.3, bf16[512,2048]{1,0:T(8,128)(2,1)S(1)} %copy-done, ...), kind=kOutput, calls=%fused_computation.59 | convolution fusion | flops 1085144576 | bytes 7346176 | tf_op jit(solution)/shard_map/dot_general | solution.py:36
  45.5 1.0 fusion.22
  46.4 6.0 %all-to-all-start.1 = ((bf16[1,16,16,512]{3,2,0,1:T(8,128)(2,1)}), bf16[1,16,16,512]{3,2,0,1:T(8,128)(2,1)S(1)}, u32[]{:S(2)}, u32[]{:S(2)}) async-start(bf16[1,16,16,512]{3,2,0,1:T(8,128)(2,1)} %bitcast.11), calls=%async_computation.1 | async-start | bytes 524288 | tf_op jit(solution)/shard_map/all_to_all | solution.py:70
  52.5 7.6 %all-to-all-done.1 = bf16[1,16,16,512]{3,2,0,1:T(8,128)(2,1)S(1)} async-done(((bf16[1,16,16,512]{3,2,0,1:T(8,128)(2,1)}), bf16[1,16,16,512]{3,2,0,1:T(8,128)(2,1)S(1)}, u32[]{:S(2)}, u32[]{:S(2)}) %all-to-all-start.1) | async-done | bytes 262176 | tf_op jit(solution)/shard_map/all_to_all | solution.py:70
  60.4 0.4 copy.20
  60.8 1.2 reshape.118
  62.0 3.8 %fusion.7 = bf16[256,512]{1,0:T(8,128)(2,1)} fusion(bf16[2048,512]{1,0:T(8,128)(2,1)} %param.12, f32[256,2048]{1,0:T(8,128)} %fusion.26, bf16[1,1,256,512]{3,2,1,0:T(8,128)(2,1)S(1)} %get-tuple-element.5), kind=kOutput, calls=%fused_computation.13 | convolution fusion | flops 541982720 | bytes 4718592 | tf_op jit(solution)/shard_map/dot_general | solution.py:29
  65.7 109.2 %reduce-scatter.4.cloned.1.call-done = f32[16,64]{1,0:T(8,128)} async-done(((f32[512,64]{1,0:T(8,128)}), f32[16,64]{1,0:T(8,128)}) %reduce-scatter.4.cloned.1.call-update) | async-done | bytes 4112
  175.0 0.8 reshape.119
  175.8 0.6 broadcast_multiply_fusion
  (22 shorter events, 0.7 us)
Async XLA Ops:
  7.2 31.5 %copy-start = (bf16[512,2048]{1,0:T(8,128)(2,1)S(1)}, bf16[512,2048]{1,0:T(8,128)(2,1)}, u32[]{:S(2)}) copy-start(bf16[512,2048]{1,0:T(8,128)(2,1)} %param.11) | copy-start | bytes 6291460
  7.2 6.1 %copy-start.2 = (bf16[4,16,512]{2,1,0:T(8,128)(2,1)S(1)}, bf16[4,16,512]{2,1,0:T(8,128)(2,1)}, u32[]{:S(2)}) copy-start(bf16[4,16,512]{2,1,0:T(8,128)(2,1)} %param.8) | copy-start | bytes 196612
  12.3 3.3 %copy-start.4 = (s32[4]{0:T(128)S(1)}, s32[4]{0:T(128)}, u32[]{:S(2)}) copy-start(s32[4]{0:T(128)} %param.9) | copy-start | bytes 52
  17.6 21.0 %copy-start.3 = (f32[512]{0:T(512)S(1)}, f32[512]{0:T(512)}, u32[]{:S(2)}) copy-start(f32[512]{0:T(512)} %param.10) | copy-start | bytes 6148
  38.7 2.2 %copy-start.1 = (bf16[1,16,16,512]{3,2,1,0:T(8,128)(2,1)S(1)}, bf16[1,16,16,512]{3,2,1,0:T(8,128)(2,1)}, u32[]{:S(2)}) copy-start(bf16[1,16,16,512]{3,2,1,0:T(8,128)(2,1)} %param.13) | copy-start | bytes 786436
  46.4 13.7 %all-to-all-start.1 = ((bf16[1,16,16,512]{3,2,0,1:T(8,128)(2,1)}), bf16[1,16,16,512]{3,2,0,1:T(8,128)(2,1)S(1)}, u32[]{:S(2)}, u32[]{:S(2)}) async-start(bf16[1,16,16,512]{3,2,0,1:T(8,128)(2,1)} %bitcast.11), calls=%async_computation.1 | async-start | bytes 524288 | tf_op jit(solution)/shard_map/all_to_all | solution.py:70
  52.5 122.5 %reduce-scatter.4.cloned.1.call-start = ((), (), s32[]{:S(2)}) async-start(), calls=%async_computation.3 | async-start | bytes 270336
Sparse Core Ops, SparseCore 0:
  62.1 112.8 reduce-scatter.3
where the time goes:
time: 184 us; the launch traced here: 183 us
  waiting for transfers between devices  117 us (64%)
  blocking collectives  17 us (9%)
  between operations  14.9 us (8%)
  matrix products  13.1 us (7%)
  local copies, waits for them, and re-layouts  9.68 us (5%)
  starting transfers between devices  6.06 us (3%)
  other arithmetic  5.72 us (3%)
    unnamed x2, waiting for transfers between devices  109 us
    all_to_all x1, blocking collectives, local(): lax.all_to_all(token_rows, 'var', split_axis=2, concat_axis=1, tiled=True)  17 us
    all_to_all x1, waiting for transfers between devices, local(): lax.all_to_all(token_gradient, 'var', split_axis=1, concat_axis=2, tiled=...  7.6 us
    all_to_all x1, starting transfers between devices, local(): lax.all_to_all(token_gradient, 'var', split_axis=1, concat_axis=2, tiled=...  6.03 us
    dot_general x1, matrix products, block_pass(): dnorm = jnp.dot(dpre, w_in.T, preferred_element_type=jnp.float32)  4.66 us
    dot_general x1, matrix products, block_pass(): jnp.dot(hidden, w_out, preferred_element_type=jnp.float32)  3.76 us
  transfers between devices with their start and end apart: 2, of which 2 were waited for; matrix products, arithmetic and copies ran while one was open for 2% of the time, Pallas kernels for 0%

commit v1 on v0

--- a/solution.py
+++ b/solution.py
@@ -67,7 +67,12 @@
     token_rows = jnp.einsum("lv,bvne->blne", own_assign, patch_embeddings).astype(jnp.bfloat16)
     row_tokens = lax.all_to_all(token_rows, "var", split_axis=2, concat_axis=1, tiled=True)
     block_out, token_gradient = block_pass(row_tokens, cotangent, norm_gain_vector, w_in, w_out)
-    dlevel = lax.all_to_all(token_gradient, "var", split_axis=1, concat_axis=2, tiled=True)
+    dlevel = jnp.concatenate(
+        lax.all_to_all(
+            jnp.stack(jnp.split(token_gradient, lax.axis_size("var"), axis=1)), "var", 0, 0
+        ),
+        axis=2,
+    )
     partial_grad = (
         jnp.einsum("bvnp,bne->vpe", patch_inputs, dlevel[:, 0], preferred_element_type=jnp.float32)
         * own_member[:, None, None]

time: 184 us -> 193 us (1.049)
  local copies, waits for them, and re-layouts: 9.68 us -> 19.4 us
    unnamed x17 -> x32, local copies, waits for them, and re-layouts: 3.43 us -> 12.5 us
where the time goes in v1:
time: 193 us; the launch traced here: 192 us
  waiting for transfers between devices  117 us (61%)
  local copies, waits for them, and re-layouts  19.4 us (10%)
  blocking collectives  17 us (9%)
  between operations  14.9 us (8%)
  matrix products  13.1 us (7%)
  starting transfers between devices  6.04 us (3%)
  other arithmetic  4.95 us (3%)
    unnamed x2, waiting for transfers between devices  109 us
    all_to_all x1, blocking collectives, local(): lax.all_to_all(token_rows, 'var', split_axis=2, concat_axis=1, tiled=True)  17 us
    unnamed x32, local copies, waits for them, and re-layouts  12.5 us
    all_to_all x1, waiting for transfers between devices, local(): lax.all_to_all(jnp.stack(jnp.split(token_gradient, lax.axis_size('var'),...  7.61 us
    all_to_all x1, starting transfers between devices, local(): lax.all_to_all(jnp.stack(jnp.split(token_gradient, lax.axis_size('var'),...  6 us
    dot_general x1, matrix products, block_pass(): dnorm = jnp.dot(dpre, w_in.T, preferred_element_type=jnp.float32)  4.64 us
  transfers between devices with their start and end apart: 2, of which 2 were waited for; matrix products, arithmetic and copies ran while one was open for 2% of the time, Pallas kernels for 0%

profile of v1, /device:TPU:2, one launch (start us, length us, event | category | flops | bytes accessed | tf_op | source)
XLA Modules:
  0.0 192.3 jit_solution(17683489372025153229)
XLA Ops:
  7.2 1.4 convert_reduce_fusion.1
  9.3 3.0 %reshape.102 = bf16[1,4,8,4,32,4]{5,4,3,2,1,0:T(8,128)(2,1)S(1)} reshape(bf16[1,4,32,128]{3,2,1,0:T(8,128)(2,1)} %param.7) | data formatting | bytes 65536 | tf_op jit(solution)/shard_map/reshape | solution.py:11
  12.3 0.9 copy.13
  13.8 1.8 copy.16
  15.6 1.9 fusion.47
  18.5 2.2 %reduce.6 = bf16[256,512]{1,0:T(8,128)(2,1)S(1)} reduce(bf16[256,1,1,512]{3,2,1,0:T(2,128)(2,1)S(1)} %bitcast.154, bf16[]{:T(256)} %broadcast.100), dimensions={1,2}, to_apply=%bitcast.150.reduce_sub_computation | reduce | bytes 524290
  20.9 17.0 %all_to_all.14 = bf16[16,2,4096]{2,1,0:T(2,128)(2,1)S(1)} all-to-all(bf16[16,2,4096]{2,1,0:T(2,128)(2,1)S(1)} %reshape.116), channel_id=1, replica_groups=mesh['var'=16,'dp'=32] {'var'}, dimensions={0} | all-to-all | bytes 524288 | tf_op jit(solution)/shard_map/all_to_all | solution.py:68
  38.6 2.2 %fusion.26 = f32[256,2048]{1,0:T(8,128)} fusion(bf16[512,2048]{1,0:T(8,128)(2,1)S(1)} %copy-done, bf16[1,1,256,512]{3,2,1,0:T(8,128)(2,1)S(1)} %get-tuple-element.5, f32[512]{0:T(512)S(1)} %copy-done.3, f32[256]{0:T(256)S(1)} %add_rsqrt_fusion, f32[256]{0:T(256)S(1)} %broadcast_multiply_fusion.3), kind=kOutput, calls=%fused_computation.35 | convolution fusion | flops 537526272 | bytes 4460544 | tf_op jit(solution)/shard_map/dot_general | solution.py:27
  40.8 4.6 %fusion.43 = (f32[256]{0:T(256)S(1)}, f32[256]{0:T(256)S(1)}, f32[256,512]{1,0:T(8,128)S(1)}) fusion(f32[256]{0:T(256)S(1)} %add_rsqrt_fusion, f32[256]{0:T(256)S(1)} %broadcast_multiply_fusion.3, bf16[1,1,256,512]{3,2,1,0:T(8,128)(2,1)S(1)} %get-tuple-element.5, f32[512]{0:T(512)S(1)} %copy-done.3, bf16[512,2048]{1,0:T(8,128)(2,1)S(1)} %copy-done, ...), kind=kOutput, calls=%fused_computation.91 | convolution fusion | flops 1085144576 | bytes 7346176 | tf_op jit(solution)/shard_map/dot_general | solution.py:36
  45.7 0.6 constant_dynamic-update-slice_fusion.15
  46.3 0.6 constant_dynamic-update-slice_fusion.14
  46.9 0.6 constant_dynamic-update-slice_fusion.13
  48.7 0.6 constant_dynamic-update-slice_fusion.10
  49.3 0.6 constant_dynamic-update-slice_fusion.9
  49.9 0.6 constant_dynamic-update-slice_fusion.8
  50.5 0.6 constant_dynamic-update-slice_fusion.7
  51.1 0.6 constant_dynamic-update-slice_fusion.6
  55.4 6.0 %all-to-all-start.1 = ((bf16[16,1,1,16,512]{4,3,2,1,0:T(8,128)(2,1)}), bf16[16,1,1,16,512]{4,3,2,1,0:T(8,128)(2,1)S(1)}, u32[]{:S(2)}, u32[]{:S(2)}) async-start(bf16[16,1,1,16,512]{4,3,2,1,0:T(8,128)(2,1)} %constant_dynamic-update-slice_fusion), calls=%async_computation.1 | async-start | bytes 524288 | tf_op jit(solution)/shard_map/all_to_all | solution.py:71
  61.4 7.6 %all-to-all-done.1 = bf16[16,1,1,16,512]{4,3,2,1,0:T(8,128)(2,1)S(1)} async-done(((bf16[16,1,1,16,512]{4,3,2,1,0:T(8,128)(2,1)}), bf16[16,1,1,16,512]{4,3,2,1,0:T(8,128)(2,1)S(1)}, u32[]{:S(2)}, u32[]{:S(2)}) %all-to-all-start.1) | async-done | bytes 262176 | tf_op jit(solution)/shard_map/all_to_all | solution.py:71
  69.7 1.2 reshape.114
  70.9 3.8 %fusion.7 = bf16[256,512]{1,0:T(8,128)(2,1)} fusion(bf16[2048,512]{1,0:T(8,128)(2,1)} %param.12, f32[256,2048]{1,0:T(8,128)} %fusion.26, bf16[1,1,256,512]{3,2,1,0:T(8,128)(2,1)S(1)} %get-tuple-element.5), kind=kOutput, calls=%fused_computation.13 | convolution fusion | flops 541982720 | bytes 4718592 | tf_op jit(solution)/shard_map/dot_general | solution.py:29
  74.7 109.3 %reduce-scatter.4.cloned.1.call-done = f32[16,64]{1,0:T(8,128)} async-done(((f32[512,64]{1,0:T(8,128)}), f32[16,64]{1,0:T(8,128)}) %reduce-scatter.4.cloned.1.call-update) | async-done | bytes 4112
  183.9 0.8 reshape.115
  184.8 0.6 broadcast_multiply_fusion
  (38 shorter events, 8.3 us)
Async XLA Ops:
  7.2 31.4 %copy-start = (bf16[512,2048]{1,0:T(8,128)(2,1)S(1)}, bf16[512,2048]{1,0:T(8,128)(2,1)}, u32[]{:S(2)}) copy-start(bf16[512,2048]{1,0:T(8,128)(2,1)} %param.11) | copy-start | bytes 6291460
  7.2 6.1 %copy-start.2 = (bf16[4,16,512]{2,1,0:T(8,128)(2,1)S(1)}, bf16[4,16,512]{2,1,0:T(8,128)(2,1)}, u32[]{:S(2)}) copy-start(bf16[4,16,512]{2,1,0:T(8,128)(2,1)} %param.8) | copy-start | bytes 196612
  12.3 3.3 %copy-start.4 = (s32[4]{0:T(128)S(1)}, s32[4]{0:T(128)}, u32[]{:S(2)}) copy-start(s32[4]{0:T(128)} %param.9) | copy-start | bytes 52
  17.6 21.0 %copy-start.3 = (f32[512]{0:T(512)S(1)}, f32[512]{0:T(512)}, u32[]{:S(2)}) copy-start(f32[512]{0:T(512)} %param.10) | copy-start | bytes 6148
  38.6 2.2 %copy-start.1 = (bf16[1,16,16,512]{3,2,1,0:T(8,128)(2,1)S(1)}, bf16[1,16,16,512]{3,2,1,0:T(8,128)(2,1)}, u32[]{:S(2)}) copy-start(bf16[1,16,16,512]{3,2,1,0:T(8,128)(2,1)} %param.13) | copy-start | bytes 786436
  55.4 13.7 %all-to-all-start.1 = ((bf16[16,1,1,16,512]{4,3,2,1,0:T(8,128)(2,1)}), bf16[16,1,1,16,512]{4,3,2,1,0:T(8,128)(2,1)S(1)}, u32[]{:S(2)}, u32[]{:S(2)}) async-start(bf16[16,1,1,16,512]{4,3,2,1,0:T(8,128)(2,1)} %constant_dynamic-update-slice_fusion), calls=%async_computation.1 | async-start | bytes 524288 | tf_op jit(solution)/shard_map/all_to_all | solution.py:71
  61.4 122.6 %reduce-scatter.4.cloned.1.call-start = ((), (), s32[]{:S(2)}) async-start(), calls=%async_computation.3 | async-start | bytes 270336
Sparse Core Ops, SparseCore 0:
  71.0 112.8 reduce-scatter.3
